TPU v7x, 512 devices: a whole 4x8x8 slice. The times are simulated.
512 devices in a mesh: dp: 64 (over z, y), seq: 8 (over x, core).
Axes of the slice: x: 4, y: 8, z: 8, core: 2. Of those that a mesh axis runs over, the one named last changes fastest.
Arguments:
- checkpoint: bfloat16 [65536, 8192], P(('dp', 'seq')), may hold values from -6 to 6
- norm_gain: float32 [8192], replicated, may hold values from 0.1 to 1.9
- key_cotangent: bfloat16 [65536, 1024], P(('dp', 'seq')), may hold values from -6 to 6
- positions: int32 [65536], P(('dp', 'seq')), may hold values from 0 to 4095, as said below
- kept_cols: int32 [128, 6], replicated, may hold values from 0 to 15, as said below
- kept_count: int32 [128], replicated, may hold values from 2 to 6
- key_blocks: bfloat16 [128, 6, 4096], P('dp'), may hold values from -0.375 to 0.375
Outputs:
- input_grad: bfloat16 [65536, 8192], P(('dp', 'seq'))
- block_grad: float32 [128, 6, 4096], P('dp', None, 'seq')
Inputs may be any that keep to these rules, and one draw needn't show every extreme that they name: `kept_cols`: the 6 entries of a row are different block columns; only the first kept_count entries of a row name kept blocks, the others are unused slots. Inside a document the positions rise by one from token to token.
All inputs are finite; a program needn't handle non-finite values.
Results may differ from a plain program's by a relative error of at most 0.0049.
Values may be sent and summed in bfloat16 or wider, within the bound.
No kernel may reach another device: no remote copies, remote signals or barrier semaphores. Data moves between devices by JAX's collectives and lax.ppermute only.
A program may use at most 128 MiB of HBM per device.

v0:
```python
import math
import jax
import jax.numpy as jnp
from jax import lax
from jax.sharding import PartitionSpec as P

D = 8192
KVW = 1024
HEAD_DIM = 128
BLK = 64
MOSTR = 6
SEQ_LEN = 1024


def rope_back(grad, positions):
    heads = KVW // HEAD_DIM
    half = HEAD_DIM // 2
    values = grad.astype(jnp.float32).reshape(-1, heads, 2, half)
    freqs = 10000.0 ** (-2.0 * jnp.arange(half).astype(jnp.float32) / HEAD_DIM)
    angle = positions.astype(jnp.float32)[:, None] * freqs[None, :]
    cosine = jnp.cos(angle)[:, None, :]
    sine = jnp.sin(angle)[:, None, :]
    first = values[:, :, 0] * cosine + values[:, :, 1] * sine
    second = values[:, :, 1] * cosine - values[:, :, 0] * sine
    return jnp.stack([first, second], axis=2).reshape(-1, KVW).astype(jnp.bfloat16)


def densify(blocks, cols, count, rows):
    count_rows = blocks.shape[0]
    col_blocks = KVW // BLK
    slot_ids = lax.broadcasted_iota(jnp.int32, (count_rows, MOSTR), 1)
    live = slot_ids < count[:, None]
    col_ids = lax.broadcasted_iota(jnp.int32, (count_rows, MOSTR, col_blocks), 2)
    onehot = ((cols[:, :, None] == col_ids) & live[:, :, None]).astype(jnp.bfloat16)
    placed = lax.dot_general(
        onehot, blocks, (((1,), (1,)), ((0,), (0,))), preferred_element_type=jnp.bfloat16
    )
    dense = placed.reshape(count_rows, col_blocks, rows, BLK).transpose(0, 2, 1, 3)
    return dense.reshape(count_rows * rows, KVW)


def shards(checkpoint, norm_gain, key_cotangent, positions, kept_cols, kept_count, key_blocks):
    tok_rows = checkpoint.shape[0]
    groups = lax.axis_size("seq")
    part_rows = BLK // groups
    row_blocks = D // BLK
    col_blocks = KVW // BLK
    xf = checkpoint.astype(jnp.float32)
    inv_rms = lax.rsqrt(jnp.mean(xf * xf, axis=1, keepdims=True) + 1e-05)
    normed = (xf * inv_rms * norm_gain).astype(jnp.bfloat16)
    grad_pre = rope_back(key_cotangent, positions)
    grad_all = lax.all_gather(grad_pre, "seq", axis=0, tiled=True)
    split_normed = (
        normed.reshape(tok_rows, row_blocks, groups, part_rows)
        .transpose(0, 2, 1, 3)
        .reshape(tok_rows, groups, row_blocks * part_rows)
    )
    received = lax.all_to_all(split_normed, "seq", split_axis=1, concat_axis=0, tiled=True)
    normed_rows = received.reshape(groups * tok_rows, row_blocks, part_rows)
    divisor = math.sqrt(SEQ_LEN * lax.axis_size("dp"))
    count = row_blocks // lax.axis_size("dp") * lax.axis_size("dp")
    slab = normed_rows.reshape(groups * tok_rows, count * part_rows)
    product = lax.dot_general(
        slab, grad_all, (((0,), (0,)), ((), ())), preferred_element_type=jnp.float32
    )
    shaped = (
        product.reshape(count, part_rows, col_blocks, BLK)
        .transpose(0, 2, 1, 3)
        .reshape(count, col_blocks, part_rows * BLK)
    )
    cols = kept_cols
    counts = kept_count
    picked = jnp.take_along_axis(shaped, cols[:, :, None], axis=1)
    live = lax.broadcasted_iota(jnp.int32, (count, MOSTR), 1) < counts[:, None]
    block_grad = lax.psum_scatter(
        jnp.where(live[:, :, None], picked / divisor, jnp.float32(0.0)),
        "dp",
        scatter_dimension=0,
        tiled=True,
    )
    piece = lax.all_gather(key_blocks, "dp", axis=0, tiled=True)
    cols = kept_cols
    counts = kept_count
    dense = densify(piece, cols, counts, BLK)
    normed_grad = lax.dot_general(
        grad_pre, dense, (((1,), (1,)), ((), ())), preferred_element_type=jnp.float32
    )
    scaled = norm_gain * normed_grad
    grads = inv_rms * scaled - inv_rms**3 * xf * jnp.mean(scaled * xf, axis=1, keepdims=True)
    return (grads.astype(jnp.bfloat16), block_grad)


def solution(mesh):
    placed = (
        P(("dp", "seq"), None),
        P(),
        P(("dp", "seq"), None),
        P(("dp", "seq")),
        P(),
        P(),
        P("dp", None, None),
    )
    return jax.shard_map(
        shards,
        mesh=mesh,
        in_specs=placed,
        out_specs=(P(("dp", "seq"), None), P("dp", None, "seq")),
        check_vma=False,
    )
```

profile of v0, /device:TPU:2, one launch (start us, length us, event | category | flops | bytes accessed | tf_op | source)
XLA Modules:
  0.0 578.3 jit_solution(3472981876656661758)
XLA Ops:
  7.2 1.6 copy.31
  9.6 1.1 copy.29
  12.5 0.8 copy.30
  13.3 102.3 %all-gather.3.cloned.1.call-done = bf16[128,6,4096]{2,1,0:T(8,128)(2,1)} async-done(((bf16[2,6,4096]{2,1,0:T(8,128)(2,1)}), bf16[128,6,4096]{2,1,0:T(8,128)(2,1)}) %all-gather.3.cloned.1.call-update) | async-done | bytes 6291472 | tf_op jit(solution)/shard_map/all_gather | solution.py:81
  115.7 14.6 %fusion.9 = bf16[128,16,4096]{2,1,0:T(8,128)(2,1)} fusion(bf16[128,6,4096]{2,1,0:T(8,128)(2,1)} %all-gather.3.cloned.1.call-done, s32[128,6]{1,0:T(8,128)S(1)} %copy.30, pred[128,6]{1,0:T(8,128)(4,1)S(1)} %iota_compare_fusion.1), kind=kOutput, calls=%fused_computation.20 | convolution fusion | flops 100687872 | bytes 23072512 | tf_op jit(solution)/shard_map/dot_general | solution.py:35
  130.2 22.6 %copy.32 = bf16[128,16,4096]{0,2,1:T(8,128)(2,1)} copy(bf16[128,16,4096]{2,1,0:T(8,128)(2,1)} %fusion.9) | data formatting | bytes 33554432 | tf_op jit(solution)/shard_map/dot_general | solution.py:35
  152.8 46.0 %copy.33 = bf16[128,64,16,64]{3,2,1,0:T(8,128)(2,1)} copy(bf16[128,64,16,64]{0,3,1,2:T(8,128)(2,1)} %bitcast.39) | data formatting | bytes 33554432 | tf_op jit(solution)/shard_map/transpose | solution.py:38
  198.8 44.3 %reshape.139 = bf16[8192,1024]{1,0:T(8,128)(2,1)} reshape(bf16[128,64,16,64]{3,2,1,0:T(8,128)(2,1)} %copy.33) | data formatting | bytes 33554432 | tf_op jit(solution)/shard_map/reshape | solution.py:39
  243.1 13.6 %fusion = (f32[128]{0:T(128)S(1)}, f32[128]{0:T(128)S(1)}, f32[128,8192]{1,0:T(8,128)}) fusion(bf16[128,8192]{1,0:T(8,128)(2,1)S(1)} %copy-done, bf16[128,1024]{0,1:T(8,128)(2,1)S(1)} %bitcast.46, bf16[8192,1024]{1,0:T(8,128)(2,1)} %reshape.139, f32[8192]{0:T(1024)S(1)} %copy-done.2), kind=kOutput, calls=%fused_computation.6 | convolution fusion | flops 2153775104 | bytes 23364608 | tf_op jit(solution)/shard_map/dot_general | solution.py:85
  256.7 6.0 %fusion.6 = (bf16[128,8192]{1,0:T(8,128)(2,1)}, bf16[128,8192]{1,0:T(8,128)(2,1)}) fusion(bf16[128,8192]{1,0:T(8,128)(2,1)S(1)} %copy-done, f32[8192]{0:T(1024)S(1)} %copy-done.2, f32[128]{0:T(128)S(1)} %get-tuple-element.14, f32[128]{0:T(128)S(1)} %get-tuple-element.17, f32[128]{0:T(128)S(1)} %get-tuple-element.15, f32[128,8192]{1,0:T(8,128)} %get-tuple-element.16), kind=kLoop, calls=%fused_computation.12 | loop fusion | flops 9437184 | bytes 10520064 | tf_op jit(solution)/shard_map/convert_element_type | solution.py:50
  262.8 3.4 copy.35
  266.2 1.7 copy.50
  267.9 4.9 all-to-all-start
  273.2 25.3 %all-to-all-done = bf16[128,8,1024]{0,2,1:T(8,128)(2,1)S(1)} async-done(((bf16[128,8,1024]{0,2,1:T(8,128)(2,1)}), bf16[128,8,1024]{0,2,1:T(8,128)(2,1)S(1)}, u32[]{:S(2)}, u32[]{:S(2)}) %all-to-all-start) | async-done | bytes 2097184 | tf_op jit(solution)/shard_map/all_to_all | solution.py:58
  298.5 2.6 copy.37
  301.1 2.9 copy.38
  304.0 4.9 convolution_bitcast_fusion
  308.9 2.3 copy.40
  311.2 5.5 copy.42
  316.7 7.5 %gather_fusion = f32[768,512]{1,0:T(8,128)S(1)} fusion(f32[128,16,512]{2,1,0:T(8,128)} %copy.42, s32[768]{0:T(1024)S(1)} %reshape.145), kind=kCustom, calls=%fused_computation | custom fusion | bytes 3151872 | tf_op jit(solution)/shard_map/jit(take_along_axis)/gather | solution.py:73
  324.2 1.5 reshape.148
  325.7 2.8 multiply_select_fusion
  328.5 241.8 %reduce-scatter.2.cloned.1.call-done = f32[2,6,512]{2,1,0:T(8,128)} async-done(((f32[128,6,512]{2,1,0:T(8,128)}), f32[2,6,512]{2,1,0:T(8,128)}) %reduce-scatter.2.cloned.1.call-update) | async-done | bytes 24592 | tf_op jit(solution)/shard_map/reduce_scatter | solution.py:75
  570.4 1.4 copy.43
  (28 shorter events, 3.0 us)
Async XLA Ops:
  7.2 108.5 %all-gather.3.cloned.1.call-start = ((), (), s32[]{:S(2)}) async-start(), calls=%async_computation.2 | async-start | bytes 8519680 | tf_op jit(solution)/shard_map/all_gather | solution.py:81
  8.8 295.1 %all-gather.5.cloned.1.call-start = ((), (), s32[]{:S(2)}) async-start(), calls=%async_computation.3 | async-start | bytes 2359296 | tf_op jit(solution)/shard_map/all_gather | solution.py:52
  198.8 44.3 %copy-start = (bf16[128,8192]{1,0:T(8,128)(2,1)S(1)}, bf16[128,8192]{1,0:T(8,128)(2,1)}, u32[]{:S(2)}) copy-start(bf16[128,8192]{1,0:T(8,128)(2,1)} %param.7) | copy-start | bytes 6291460
  198.8 44.3 %copy-start.1 = (bf16[128,8,2,64]{0,3,2,1:T(8,128)(2,1)S(1)}, bf16[128,8,2,64]{0,3,2,1:T(8,128)(2,1)}, u32[]{:S(2)}) copy-start(bf16[128,8,2,64]{0,3,2,1:T(8,128)(2,1)} %maximum_convert_fusion) | copy-start | bytes 786436
  198.8 44.3 %copy-start.2 = (f32[8192]{0:T(1024)S(1)}, f32[8192]{0:T(1024)}, u32[]{:S(2)}) copy-start(f32[8192]{0:T(1024)} %param.8) | copy-start | bytes 98308
  266.2 6.6 %copy-start.3 = (s32[128,6]{0,1:T(8,128)S(1)}, s32[128,6]{0,1:T(8,128)}, u32[]{:S(2)}) copy-start(s32[128,6]{0,1:T(8,128)} %param.11) | copy-start | bytes 9220
  267.9 30.6 %all-to-all-start = ((bf16[128,8,1024]{0,2,1:T(8,128)(2,1)}), bf16[128,8,1024]{0,2,1:T(8,128)(2,1)S(1)}, u32[]{:S(2)}, u32[]{:S(2)}) async-start(bf16[128,8,1024]{0,2,1:T(8,128)(2,1)} %bitcast.42), calls=%async_computation | async-start | bytes 4194304 | tf_op jit(solution)/shard_map/all_to_all | solution.py:58
  272.8 297.6 %reduce-scatter.2.cloned.1.call-start = ((), (), s32[]{:S(2)}) async-start(), calls=%async_computation.4 | async-start | bytes 2129920 | tf_op jit(solution)/shard_map/reduce_scatter | solution.py:75
Sparse Core Ops, SparseCore 0:
  11.6 103.9 all-gather.2
  117.8 30.1 all-gather.4
  328.7 241.6 reduce-scatter.1
where the time goes:
time: 582 us; the launch traced here: 578 us
  waiting for transfers between devices  370 us (64%)
  local copies, waits for them, and re-layouts  146 us (25%)
  matrix products  33.1 us (6%)
  between operations  13.9 us (2%)
  other arithmetic  11.3 us (2%)
    reduce_scatter x1, waiting for transfers between devices, shards(): lax.psum_scatter(jnp.where(live[:, :, None], picked / divisor, jnp.float3...  242 us
    all_gather x1, waiting for transfers between devices, shards(): piece = lax.all_gather(key_blocks, 'dp', axis=0, tiled=True)  102 us
    transpose x1, local copies, waits for them, and re-layouts, densify(): placed.reshape(count_rows, col_blocks, rows, BLK).transpose(0, 2, 1, 3)  46 us
    reshape x1, local copies, waits for them, and re-layouts, densify(): return dense.reshape(count_rows * rows, KVW)  44.3 us
    all_to_all x1, waiting for transfers between devices, shards(): lax.all_to_all(split_normed, 'seq', split_axis=1, concat_axis=0, tiled=True)  25.3 us
    dot_general x1, local copies, waits for them, and re-layouts, densify(): lax.dot_general(onehot, blocks, (((1,), (1,)), ((0,), (0,))), preferred_e...  22.6 us
    dot_general x1, matrix products, densify(): lax.dot_general(onehot, blocks, (((1,), (1,)), ((0,), (0,))), preferred_e...  14.6 us
    dot_general x1, matrix products, shards(): lax.dot_general(grad_pre, dense, (((1,), (1,)), ((), ())), preferred_elem...  13.6 us
  transfers between devices with their start and end apart: 4, of which 3 were waited for; matrix products, arithmetic and copies ran while one was open for 28% of the time, Pallas kernels for 0%

commit v1 on v0

--- a/solution.py
+++ b/solution.py
@@ -10,6 +10,13 @@
 BLK = 64
 MOSTR = 6
 SEQ_LEN = 1024
+
+
+def swapped_in(shard, axis, dim):
+    n_dev = lax.axis_size(axis)
+    tiles = jnp.stack([shard for _ in range(n_dev)])
+    tiles = lax.all_to_all(tiles, axis, split_axis=0, concat_axis=0)
+    return jnp.concatenate(tiles, axis=dim)
 
 
 def rope_back(grad, positions):
@@ -78,7 +85,7 @@
         scatter_dimension=0,
         tiled=True,
     )
-    piece = lax.all_gather(key_blocks, "dp", axis=0, tiled=True)
+    piece = swapped_in(key_blocks, "dp", 0)
     cols = kept_cols
     counts = kept_count
     dense = densify(piece, cols, counts, BLK)

time: 582 us -> 707 us (1.21)
  waiting for transfers between devices: 370 us -> 470 us
  starting transfers between devices: 4.95 us -> 21.8 us
  local copies, waits for them, and re-layouts: 146 us -> 157 us
    all_to_all x0 -> x1, waiting for transfers between devices: none -> 167 us  [swapped_in(): tiles = lax.all_to_all(tiles, axis, split_axis=0, concat_axis=0)]
    all_gather x1 -> x0, waiting for transfers between devices: 102 us -> none  [shards(): piece = lax.all_gather(key_blocks, 'dp', axis=0, tiled=True)]
    reduce_scatter x1, waiting for transfers between devices: 242 us -> 277 us  [shards(): lax.psum_scatter(jnp.where(live[:, :, None], picked / divisor, jnp.float3...]
    all_to_all x0 -> x1, starting transfers between devices: none -> 17 us  [swapped_in(): tiles = lax.all_to_all(tiles, axis, split_axis=0, concat_axis=0)]
    all_to_all x0 -> x1, local copies, waits for them, and re-layouts: none -> 10.2 us  [swapped_in(): tiles = lax.all_to_all(tiles, axis, split_axis=0, concat_axis=0)]
  transfers between devices with their start and end apart: 4 -> 4, of which waited for: 3 -> 3; matrix products, arithmetic and copies ran while one was open for 28% -> 24% of each run, Pallas kernels for 0% -> 0%
where the time goes in v1:
time: 707 us; the launch traced here: 703 us
  waiting for transfers between devices  470 us (66%)
  local copies, waits for them, and re-layouts  157 us (22%)
  matrix products  30.2 us (4%)
  starting transfers between devices  21.8 us (3%)
  between operations  14.2 us (2%)
  other arithmetic  9.99 us (1%)
    reduce_scatter x1, waiting for transfers between devices, shards(): lax.psum_scatter(jnp.where(live[:, :, None], picked / divisor, jnp.float3...  277 us
    all_to_all x1, waiting for transfers between devices, swapped_in(): tiles = lax.all_to_all(tiles, axis, split_axis=0, concat_axis=0)  167 us
    transpose x1, local copies, waits for them, and re-layouts, densify(): placed.reshape(count_rows, col_blocks, rows, BLK).transpose(0, 2, 1, 3)  46 us
    reshape x1, local copies, waits for them, and re-layouts, densify(): return dense.reshape(count_rows * rows, KVW)  44.3 us
    all_to_all x1, waiting for transfers between devices, shards(): lax.all_to_all(split_normed, 'seq', split_axis=1, concat_axis=0, tiled=True)  25.3 us
    dot_general x1, local copies, waits for them, and re-layouts, densify(): lax.dot_general(onehot, blocks, (((1,), (1,)), ((0,), (0,))), preferred_e...  22.5 us
    all_to_all x1, starting transfers between devices, swapped_in(): tiles = lax.all_to_all(tiles, axis, split_axis=0, concat_axis=0)  17 us
  transfers between devices with their start and end apart: 4, of which 3 were waited for; matrix products, arithmetic and copies ran while one was open for 24% of the time, Pallas kernels for 0%

profile of v1, /device:TPU:2, one launch (start us, length us, event | category | flops | bytes accessed | tf_op | source)
XLA Modules:
  0.0 703.1 jit_solution(5472048976500251336)
XLA Ops:
  7.2 5.1 stack.5
  12.3 17.0 %all-to-all-start = ((bf16[64,2,6,4096]{3,1,2,0:T(2,128)(2,1)}), bf16[64,2,6,4096]{3,1,2,0:T(2,128)(2,1)}, u32[]{:S(2)}, u32[]{:S(2)}) async-start(bf16[64,2,6,4096]{3,1,2,0:T(2,128)(2,1)} %stack.5), calls=%async_computation | async-start | bytes 12582912 | tf_op jit(solution)/shard_map/all_to_all | solution.py:18
  30.8 167.3 %all-to-all-done = bf16[64,2,6,4096]{3,1,2,0:T(2,128)(2,1)} async-done(((bf16[64,2,6,4096]{3,1,2,0:T(2,128)(2,1)}), bf16[64,2,6,4096]{3,1,2,0:T(2,128)(2,1)}, u32[]{:S(2)}, u32[]{:S(2)}) %all-to-all-start) | async-done | bytes 6291488 | tf_op jit(solution)/shard_map/all_to_all | solution.py:18
  198.1 10.2 %copy.31 = bf16[64,2,6,4096]{3,2,1,0:T(8,128)(2,1)S(1)} copy(bf16[64,2,6,4096]{3,1,2,0:T(2,128)(2,1)} %all-to-all-done) | data formatting | bytes 12582912 | tf_op jit(solution)/shard_map/all_to_all | solution.py:18
  208.3 11.7 %fusion.9 = bf16[128,16,4096]{2,1,0:T(8,128)(2,1)} fusion(bf16[128,6,4096]{2,1,0:T(8,128)(2,1)S(1)} %bitcast.41, s32[128,6]{1,0:T(8,128)S(1)} %copy.30, pred[128,6]{1,0:T(8,128)(4,1)S(1)} %iota_compare_fusion.1), kind=kOutput, calls=%fused_computation.20 | convolution fusion | flops 100687872 | bytes 23072512 | tf_op jit(solution)/shard_map/dot_general | solution.py:42
  220.0 22.5 %copy.32 = bf16[128,16,4096]{0,2,1:T(8,128)(2,1)} copy(bf16[128,16,4096]{2,1,0:T(8,128)(2,1)} %fusion.9) | data formatting | bytes 33554432 | tf_op jit(solution)/shard_map/dot_general | solution.py:42
  242.5 46.0 %copy.33 = bf16[128,64,16,64]{3,2,1,0:T(8,128)(2,1)} copy(bf16[128,64,16,64]{0,3,1,2:T(8,128)(2,1)} %bitcast.40) | data formatting | bytes 33554432 | tf_op jit(solution)/shard_map/transpose | solution.py:45
  288.4 44.3 %reshape.145 = bf16[8192,1024]{1,0:T(8,128)(2,1)} reshape(bf16[128,64,16,64]{3,2,1,0:T(8,128)(2,1)} %copy.33) | data formatting | bytes 33554432 | tf_op jit(solution)/shard_map/reshape | solution.py:46
  332.7 13.6 %fusion = (f32[128]{0:T(128)S(1)}, f32[128]{0:T(128)S(1)}, f32[128,8192]{1,0:T(8,128)}) fusion(bf16[128,8192]{1,0:T(8,128)(2,1)S(1)} %copy-done, bf16[128,1024]{0,1:T(8,128)(2,1)S(1)} %bitcast.48, bf16[8192,1024]{1,0:T(8,128)(2,1)} %reshape.145, f32[8192]{0:T(1024)S(1)} %copy-done.3), kind=kOutput, calls=%fused_computation.6 | convolution fusion | flops 2153775104 | bytes 23364608 | tf_op jit(solution)/shard_map/dot_general | solution.py:92
  346.4 6.0 fusion.6
  352.4 3.2 copy.35
  355.6 1.7 copy.50
  357.3 4.8 all-to-all-start.1
  362.6 25.3 %all-to-all-done.1 = bf16[128,8,1024]{0,2,1:T(8,128)(2,1)S(1)} async-done(((bf16[128,8,1024]{0,2,1:T(8,128)(2,1)}), bf16[128,8,1024]{0,2,1:T(8,128)(2,1)S(1)}, u32[]{:S(2)}, u32[]{:S(2)}) %all-to-all-start.1) | async-done | bytes 2097184 | tf_op jit(solution)/shard_map/all_to_all | solution.py:65
  387.9 2.6 copy.37
  390.5 2.9 copy.38
  393.4 4.9 convolution_bitcast_fusion
  398.3 2.3 copy.40
  400.6 5.5 copy.42
  406.1 7.5 %gather_fusion = f32[768,512]{1,0:T(8,128)S(1)} fusion(f32[128,16,512]{2,1,0:T(8,128)} %copy.42, s32[768]{0:T(1024)S(1)} %reshape.151), kind=kCustom, calls=%fused_computation | custom fusion | bytes 3151872 | tf_op jit(solution)/shard_map/jit(take_along_axis)/gather | solution.py:80
  413.6 1.5 reshape.154
  415.1 2.8 multiply_select_fusion
  417.9 277.0 %reduce-scatter.2.cloned.1.call-done = f32[2,6,512]{2,1,0:T(8,128)} async-done(((f32[128,6,512]{2,1,0:T(8,128)}), f32[2,6,512]{2,1,0:T(8,128)}) %reduce-scatter.2.cloned.1.call-update) | async-done | bytes 24592 | tf_op jit(solution)/shard_map/reduce_scatter | solution.py:82
  694.9 1.4 copy.43
  (34 shorter events, 2.0 us)
Async XLA Ops:
  12.2 17.0 %copy-start.6 = (s32[128]{0:T(128)S(1)}, s32[128]{0:T(128)}, u32[]{:S(2)}) copy-start(s32[128]{0:T(128)} %param.10) | copy-start | bytes 1540
  12.2 17.1 %copy-start.2 = (bf16[128,1024]{1,0:T(8,128)(2,1)S(1)}, bf16[128,1024]{1,0:T(8,128)(2,1)}, u32[]{:S(2)}) copy-start(bf16[128,1024]{1,0:T(8,128)(2,1)} %param.9) | copy-start | bytes 786436
  12.2 18.4 %copy-start.4 = (s32[128,6]{0,1:T(8,128)S(1)}, s32[128,6]{0,1:T(8,128)}, u32[]{:S(2)}) copy-start(s32[128,6]{0,1:T(8,128)} %param.11) | copy-start | bytes 9220
  12.2 18.5 %copy-start.5 = (s32[128]{0:T(128)S(1)}, s32[128]{0:T(128)}, u32[]{:S(2)}) copy-start(s32[128]{0:T(128)} %param.12) | copy-start | bytes 1540
  12.3 185.9 %all-to-all-start = ((bf16[64,2,6,4096]{3,1,2,0:T(2,128)(2,1)}), bf16[64,2,6,4096]{3,1,2,0:T(2,128)(2,1)}, u32[]{:S(2)}, u32[]{:S(2)}) async-start(bf16[64,2,6,4096]{3,1,2,0:T(2,128)(2,1)} %stack.5), calls=%async_computation | async-start | bytes 12582912 | tf_op jit(solution)/shard_map/all_to_all | solution.py:18
  29.2 364.2 %all-gather.2.cloned.1.call-start = ((), (), s32[]{:S(2)}) async-start(), calls=%async_computation.3 | async-start | bytes 2359296 | tf_op jit(solution)/shard_map/all_gather | solution.py:59
  288.4 44.3 %copy-start = (bf16[128,8192]{1,0:T(8,128)(2,1)S(1)}, bf16[128,8192]{1,0:T(8,128)(2,1)}, u32[]{:S(2)}) copy-start(bf16[128,8192]{1,0:T(8,128)(2,1)} %param.7) | copy-start | bytes 6291460
  288.4 44.3 %copy-start.1 = (bf16[128,8,2,64]{0,3,2,1:T(8,128)(2,1)S(1)}, bf16[128,8,2,64]{0,3,2,1:T(8,128)(2,1)}, u32[]{:S(2)}) copy-start(bf16[128,8,2,64]{0,3,2,1:T(8,128)(2,1)} %maximum_convert_fusion) | copy-start | bytes 786436
  288.4 44.3 %copy-start.3 = (f32[8192]{0:T(1024)S(1)}, f32[8192]{0:T(1024)}, u32[]{:S(2)}) copy-start(f32[8192]{0:T(1024)} %param.8) | copy-start | bytes 98308
  357.3 30.6 %all-to-all-start.1 = ((bf16[128,8,1024]{0,2,1:T(8,128)(2,1)}), bf16[128,8,1024]{0,2,1:T(8,128)(2,1)S(1)}, u32[]{:S(2)}, u32[]{:S(2)}) async-start(bf16[128,8,1024]{0,2,1:T(8,128)(2,1)} %bitcast.44), calls=%async_computation.1 | async-start | bytes 4194304 | tf_op jit(solution)/shard_map/all_to_all | solution.py:65
  362.2 332.7 %reduce-scatter.2.cloned.1.call-start = ((), (), s32[]{:S(2)}) async-start(), calls=%async_computation.4 | async-start | bytes 2129920 | tf_op jit(solution)/shard_map/reduce_scatter | solution.py:82
Sparse Core Ops, SparseCore 0:
  32.2 32.7 all-gather.1
  418.1 276.7 reduce-scatter.1
